TPU v7x, 128 devices: a whole 4x4x4 slice. The times are simulated.
128 devices in a mesh: seq: 16 (over z_lo, y, core), head: 8 (over z_hi, x).
Axes of the slice: x: 4, y: 4, z: 4 (z_hi: 2, z_lo: 2; z = z_hi * 2 + z_lo), core: 2. Of those that a mesh axis runs over, the one named last changes fastest.
Arguments:
- inputs: bfloat16 [16384, 5376], P(('seq', 'head')), may hold values from -18 to 18
- queries: bfloat16 [16384, 4096], P('seq', 'head'), may hold values from -12 to 12
- key_rows: bfloat16 [16384, 2048], P('seq', 'head'), may hold values from -12 to 12
- values: bfloat16 [16384, 2048], P('seq', 'head'), may hold values from -6 to 6
- out_grad: bfloat16 [16384, 4096], P('seq', 'head'), may hold values from -6 to 6
- band_start: int32 [16384], P('seq'), may hold values from 0 to 16383, as said below
- owners: int32 [8, 6], replicated, may hold values from 0 to 15, as said below
Outputs:
- left_stat: float32 [16, 8, 1024, 1024], P('seq', 'head')
- right_stat: float32 [16, 8, 1024, 1024], P('seq', 'head')
Inputs may be any that keep to these rules, and one draw needn't show every extreme that they name: band_start[i] lies between i - 1023 and i, and never decreases with i. `owners`: the 6 entries of a row differ.
All inputs are finite; a program needn't handle non-finite values.
Results may differ from a plain program's by a relative error of at most 0.015.
Values may be sent and summed in bfloat16 or wider, within the bound.
No kernel may reach another device: no remote copies, remote signals or barrier semaphores. Data moves between devices by JAX's collectives and lax.ppermute only.
A program may use at most 128 MiB of HBM per device.

v0:
```python
import jax
import jax.numpy as jnp
from jax import lax
from jax.sharding import PartitionSpec as P

D = 5376
HD = 128
KV_DEV = 2
QPK = 2
WINDOW = 1024
BLOCK = 1024
NBLK = 6


score_scale = 168.0 ** (-0.5)
rotary_frequency_base = 10000.0
neg_large = -1e30


def shifted(value, axis, steps):
    count = lax.axis_size(axis)
    initial, last = (max(0, -steps), min(count, count - steps))
    return lax.ppermute(value, axis, [(source, source + steps) for source in range(initial, last)])


def rope_tables(positions, head_size):
    half_size = head_size // 2
    frequency = jnp.power(
        rotary_frequency_base, -2.0 * jnp.arange(half_size, dtype=jnp.float32) / head_size
    )
    angles = positions.astype(jnp.float32)[:, None] * frequency[None, :]
    cosine_table = jnp.concatenate([jnp.cos(angles), jnp.cos(angles)], 1)
    sine_table = jnp.concatenate([jnp.sin(angles), jnp.sin(angles)], 1)
    return (cosine_table, sine_table)


def unrotate(gradient, cosine_table, sine_table):
    half_size = gradient.shape[-1] // 2
    scaled = gradient * sine_table
    turned = jnp.concatenate([-scaled[..., half_size:], scaled[..., :half_size]], -1)
    return gradient * cosine_table - turned


def per_device(inputs, queries, key_rows, values, out_grad, band_start, owners):
    tok_rows = queries.shape[0]
    seq_count = lax.axis_size("seq")
    seq_index = lax.axis_index("seq")
    group_index = lax.axis_index("head")
    tokens_all = tok_rows * seq_count
    earlier_keys, earlier_values = shifted((key_rows, values), "seq", 1)
    gathered_key_rows = jnp.concatenate([earlier_keys, key_rows], 0).reshape(
        2 * tok_rows, KV_DEV, HD
    )
    value_all = jnp.concatenate([earlier_values, values], 0).reshape(2 * tok_rows, KV_DEV, HD)
    query_heads = queries.reshape(tok_rows, KV_DEV, QPK, HD)
    out_heads = out_grad.reshape(tok_rows, KV_DEV, QPK, HD)
    block_rows = min(512, tok_rows)
    span_rows = block_rows + WINDOW
    block_count = tok_rows // block_rows

    def one_block(block_index, state_pair):
        grad_query, grad_keys, grad_values = state_pair
        offset = block_index * block_rows
        query_part = lax.dynamic_slice_in_dim(query_heads, offset, block_rows, 0)
        out_part = lax.dynamic_slice_in_dim(out_heads, offset, block_rows, 0)
        key_start = tok_rows + offset - WINDOW
        key_part = lax.dynamic_slice_in_dim(gathered_key_rows, key_start, span_rows, 0)
        value_part = lax.dynamic_slice_in_dim(value_all, key_start, span_rows, 0)
        band_part = lax.dynamic_slice_in_dim(band_start, offset, block_rows, 0)
        query_pos = seq_index * tok_rows + offset + jnp.arange(block_rows, dtype=jnp.int32)
        key_pos = seq_index * tok_rows + offset - WINDOW + jnp.arange(span_rows, dtype=jnp.int32)
        allowed = (key_pos[None, :] >= band_part[:, None]) & (
            key_pos[None, :] <= query_pos[:, None]
        )
        attention_logits = (
            jnp.einsum("qgrh,kgh->grqk", query_part, key_part, preferred_element_type=jnp.float32)
            * score_scale
        )
        masked = jnp.where(allowed, attention_logits, neg_large)
        row_top = jnp.max(masked, -1, keepdims=True)
        exponent = jnp.where(allowed, jnp.exp(masked - row_top), 0.0)
        attend = exponent / jnp.sum(exponent, -1, keepdims=True)
        attend_low = attend.astype(jnp.bfloat16)
        grad_attend = jnp.einsum(
            "qgrh,kgh->grqk", out_part, value_part, preferred_element_type=jnp.float32
        )
        row_dot = jnp.sum(attend * grad_attend, -1, keepdims=True)
        grad_score = (attend * (grad_attend - row_dot) * score_scale).astype(jnp.bfloat16)
        query_term = jnp.einsum(
            "grqk,kgh->qgrh", grad_score, key_part, preferred_element_type=jnp.float32
        )
        key_term = jnp.einsum(
            "grqk,qgrh->kgh", grad_score, query_part, preferred_element_type=jnp.float32
        )
        value_term = jnp.einsum(
            "grqk,qgrh->kgh", attend_low, out_part, preferred_element_type=jnp.float32
        )
        grad_query = lax.dynamic_update_slice_in_dim(grad_query, query_term, offset, 0)
        grad_keys = lax.dynamic_update_slice_in_dim(
            grad_keys,
            lax.dynamic_slice_in_dim(grad_keys, key_start, span_rows, 0) + key_term,
            key_start,
            0,
        )
        grad_values = lax.dynamic_update_slice_in_dim(
            grad_values,
            lax.dynamic_slice_in_dim(grad_values, key_start, span_rows, 0) + value_term,
            key_start,
            0,
        )
        return (grad_query, grad_keys, grad_values)

    start_state = (
        jnp.zeros((tok_rows, KV_DEV, QPK, HD), jnp.float32),
        jnp.zeros((2 * tok_rows, KV_DEV, HD), jnp.float32),
        jnp.zeros((2 * tok_rows, KV_DEV, HD), jnp.float32),
    )
    grad_query, grad_keys, grad_values = lax.fori_loop(0, block_count, one_block, start_state)
    rim_keys, rim_values = (
        shifted(grad_keys[:tok_rows].astype(jnp.bfloat16), "seq", -1).astype(jnp.float32),
        shifted(grad_values[:tok_rows].astype(jnp.bfloat16), "seq", -1).astype(jnp.float32),
    )
    own_keys = grad_keys[tok_rows:] + rim_keys
    own_values = grad_values[tok_rows:] + rim_values
    positions = seq_index * tok_rows + jnp.arange(tok_rows, dtype=jnp.int32)
    cosine_table, sine_table = rope_tables(positions, HD)
    query_pre = unrotate(
        grad_query.reshape(tok_rows, KV_DEV * QPK, HD),
        cosine_table[:, None, :],
        sine_table[:, None, :],
    )
    key_pre = unrotate(own_keys, cosine_table[:, None, :], sine_table[:, None, :])
    column_grads = jnp.concatenate(
        [
            query_pre.reshape(tok_rows, KV_DEV * QPK * HD),
            key_pre.reshape(tok_rows, KV_DEV * HD),
            own_values.reshape(tok_rows, KV_DEV * HD),
        ],
        1,
    ).astype(jnp.bfloat16)
    column_count = column_grads.shape[1]
    partial_sum = lax.dot_general(
        lax.all_gather(inputs, "head", axis=0, tiled=True),
        column_grads,
        (((0,), (0,)), ((), ())),
        preferred_element_type=jnp.float32,
    )
    gradient = lax.psum(partial_sum.astype(jnp.bfloat16), "seq")
    padded = jnp.pad(gradient, ((0, NBLK * BLOCK - D), (0, 0)))
    owner_row = lax.dynamic_index_in_dim(owners, group_index, 0, keepdims=False)
    is_mine = owner_row == seq_index
    block_pick = jnp.sum(jnp.where(is_mine, jnp.arange(NBLK, dtype=jnp.int32), 0))
    block_part = lax.dynamic_slice_in_dim(padded, block_pick * BLOCK, BLOCK, 0)

    def gram_pair(part_rows):
        left_value = (
            lax.dot_general(
                part_rows, part_rows, (((1,), (1,)), ((), ())), preferred_element_type=jnp.float32
            )
            / tokens_all
        )
        right_value = (
            lax.dot_general(
                part_rows, part_rows, (((0,), (0,)), ((), ())), preferred_element_type=jnp.float32
            )
            / tokens_all
        )
        return (left_value, right_value)

    def nothing(part_rows):
        return (
            jnp.zeros((BLOCK, BLOCK), jnp.float32),
            jnp.zeros((column_count, column_count), jnp.float32),
        )

    left_stat, right_stat = lax.cond(jnp.any(is_mine), gram_pair, nothing, block_part)
    return (left_stat[None, None], right_stat[None, None])


def solution(mesh):
    in_specs = (
        P(("seq", "head"), None),
        P("seq", "head"),
        P("seq", "head"),
        P("seq", "head"),
        P("seq", "head"),
        P("seq"),
        P(),
    )
    out_specs = (P("seq", "head", None, None), P("seq", "head", None, None))
    return jax.shard_map(
        per_device, mesh=mesh, in_specs=in_specs, out_specs=out_specs, check_vma=False
    )
```

profile of v0, /device:TPU:0, one launch (start us, length us, event | category | flops | bytes accessed | tf_op | source)
XLA Modules:
  0.0 395.2 jit_solution(2199822234930943391)
XLA Ops:
  7.2 0.7 all-gather.2.cloned.1.call-update
  8.0 1.2 copy.26
  9.2 2.1 collective-permute-start
  11.3 1.2 copy.29
  12.5 3.6 collective-permute-start.1
  16.2 1.0 multiply_cosine_fusion
  17.2 1.3 copy.28
  18.5 2.3 copy.31
  20.8 0.9 pad_maximum_fusion.4
  21.6 0.9 pad_maximum_fusion.3
  22.5 2.2 pad_maximum_fusion.1
  24.8 1.6 broadcast.83
  26.3 1.6 broadcast.83.clone
  27.9 1.6 broadcast_in_dim.95
  29.5 138.9 %while.22 = (s32[]{:T(128)}, f32[1024,2,2,128]{0,3,2,1:T(8,128)}, f32[2048,2,128]{0,2,1:T(8,128)}, f32[2048,2,128]{0,2,1:T(8,128)}, bf16[2048,2,128]{0,2,1:T(8,1...) while((s32[]{:T(128)}, f32[1024,2,2,128]{0,3,2,1:T(8,128)}, ...), condition=%wide.region_5.6_spmd, body=%wide.region_1.5_spmd.sunk | while | flops 4095748608 | bytes 186194320 | solution.py:118
  29.6 0.7 compare_and_fusion.2
  30.2 11.8 %fusion.115 = (f32[2,2,512]{2,1,0:T(2,128)S(1)}, f32[2,2,512,1536]{2,3,1,0:T(8,128)}) fusion(pred[512,1536]{0,1:T(8,128)(4,1)S(1)} %compare_and_fusion.2, bf16[2048,2,128]{0,2,1:T(8,128)(2,1)} %get-tuple-element.555, s32[]{:T(128)S(6)} %select_n.101, bf16[1024,2,2,128]{0,3,2,1:T(8,128)(2,1)} %get-tuple-element.558, s32[]{:T(128)S(6)} %select_n.100), kind=kOutput, calls=%fused_computation.99.clone.1 | convolution fusion | flops 821036544 | bytes 15474696 | tf_op jit(solution)/shard_map/while/body/eval_jaxpr/sub | solution.py:81
  42.0 7.6 %fusion.114 = f32[2,1536,512,2]{2,1,3,0:T(8,128)} fusion(bf16[2048,2,128]{0,2,1:T(8,128)(2,1)S(1)} %get-tuple-element.559, s32[]{:T(128)S(6)} %select_n.101, bf16[1024,2,2,128]{0,3,2,1:T(8,128)(2,1)} %get-tuple-element.560, s32[]{:T(128)S(6)} %select_n.100), kind=kOutput, calls=%fused_computation.33.clone.1 | convolution fusion | flops 805306368 | bytes 13893640 | tf_op jit(solution)/shard_map/while/body/eval_jaxpr/qgrh,kgh->grqk/dot_general | solution.py:84
  49.6 20.2 %fusion.117 = f32[2048,2,128]{0,2,1:T(8,128)S(1)} fusion(f32[2048,2,128]{0,2,1:T(8,128)S(1)} %copy-done.4, s32[]{:T(128)S(6)} %select_n.101, f32[2,1536,512,2]{2,1,3,0:T(8,128)} %fusion.114, bf16[1024,2,2,128]{0,3,2,1:T(8,128)(2,1)} %get-tuple-element.558, s32[]{:T(128)S(6)} %select_n.100, f32[2,2,512,1536]{2,3,1,0:T(8,128)} %get-tuple-element.517, ...), kind=kOutput, calls=%fused_computation.25.clone.1 | convolution fusion | flops 827723264 | bytes 54018056 | tf_op jit(solution)/shard_map/while/body/eval_jaxpr/grqk,qgrh->kgh/dot_general | solution.py:92
  69.8 1.3 copy-done.5
  71.1 8.7 %fusion.118 = f32[2048,2,128]{0,2,1:T(8,128)} fusion(f32[2048,2,128]{0,2,1:T(8,128)} %get-tuple-element.538, s32[]{:T(128)S(6)} %select_n.101, bf16[1024,2,2,128]{0,3,2,1:T(8,128)(2,1)} %get-tuple-element.560, s32[]{:T(128)S(6)} %select_n.100, f32[2,2,512,1536]{2,3,1,0:T(8,128)} %get-tuple-element.517, f32[2,2,512]{2,1,0:T(2,128)S(1)} %get-tuple-element.518), kind=kOutput, calls=%fused_computation.22.clone.1 | convolution fusion | flops 811991040 | bytes 16261128 | tf_op jit(solution)/shard_map/while/body/eval_jaxpr/grqk,qgrh->kgh/dot_general | solution.py:95
  79.8 17.7 %fusion.116 = f32[1024,2,2,128]{0,3,2,1:T(8,128)S(1)} fusion(f32[1024,2,2,128]{0,3,2,1:T(8,128)S(1)} %copy-done.1, s32[]{:T(128)S(6)} %select_n.100, f32[2,1536,512,2]{2,1,3,0:T(8,128)} %fusion.114, bf16[2048,2,128]{0,2,1:T(8,128)(2,1)} %get-tuple-element.555, s32[]{:T(128)S(6)} %select_n.101, f32[2,2,512,1536]{2,3,1,0:T(8,128)} %get-tuple-element.517, ...), kind=kOutput, calls=%fused_computation.27.clone.1 | convolution fusion | flops 827330048 | bytes 52183048 | tf_op jit(solution)/shard_map/while/body/eval_jaxpr/grqk,kgh->qgrh/dot_general | solution.py:89
  97.6 1.3 copy-done.2
  99.0 0.7 compare_and_fusion.2
  99.6 11.7 %fusion.115 = (f32[2,2,512]{2,1,0:T(2,128)S(1)}, f32[2,2,512,1536]{2,3,1,0:T(8,128)}) fusion(pred[512,1536]{0,1:T(8,128)(4,1)S(1)} %compare_and_fusion.2, bf16[2048,2,128]{0,2,1:T(8,128)(2,1)} %get-tuple-element.555, s32[]{:T(128)S(6)} %select_n.101, bf16[1024,2,2,128]{0,3,2,1:T(8,128)(2,1)} %get-tuple-element.558, s32[]{:T(128)S(6)} %select_n.100), kind=kOutput, calls=%fused_computation.99.clone.1 | convolution fusion | flops 821036544 | bytes 15474696 | tf_op jit(solution)/shard_map/while/body/eval_jaxpr/sub | solution.py:81
  111.4 7.6 %fusion.114 = f32[2,1536,512,2]{2,1,3,0:T(8,128)} fusion(bf16[2048,2,128]{0,2,1:T(8,128)(2,1)S(1)} %get-tuple-element.559, s32[]{:T(128)S(6)} %select_n.101, bf16[1024,2,2,128]{0,3,2,1:T(8,128)(2,1)} %get-tuple-element.560, s32[]{:T(128)S(6)} %select_n.100), kind=kOutput, calls=%fused_computation.33.clone.1 | convolution fusion | flops 805306368 | bytes 13893640 | tf_op jit(solution)/shard_map/while/body/eval_jaxpr/qgrh,kgh->grqk/dot_general | solution.py:84
  118.9 20.2 %fusion.117 = f32[2048,2,128]{0,2,1:T(8,128)S(1)} fusion(f32[2048,2,128]{0,2,1:T(8,128)S(1)} %copy-done.4, s32[]{:T(128)S(6)} %select_n.101, f32[2,1536,512,2]{2,1,3,0:T(8,128)} %fusion.114, bf16[1024,2,2,128]{0,3,2,1:T(8,128)(2,1)} %get-tuple-element.558, s32[]{:T(128)S(6)} %select_n.100, f32[2,2,512,1536]{2,3,1,0:T(8,128)} %get-tuple-element.517, ...), kind=kOutput, calls=%fused_computation.25.clone.1 | convolution fusion | flops 827723264 | bytes 54018056 | tf_op jit(solution)/shard_map/while/body/eval_jaxpr/grqk,qgrh->kgh/dot_general | solution.py:92
  139.2 1.3 copy-done.5
  140.5 8.7 %fusion.118 = f32[2048,2,128]{0,2,1:T(8,128)} fusion(f32[2048,2,128]{0,2,1:T(8,128)} %get-tuple-element.538, s32[]{:T(128)S(6)} %select_n.101, bf16[1024,2,2,128]{0,3,2,1:T(8,128)(2,1)} %get-tuple-element.560, s32[]{:T(128)S(6)} %select_n.100, f32[2,2,512,1536]{2,3,1,0:T(8,128)} %get-tuple-element.517, f32[2,2,512]{2,1,0:T(2,128)S(1)} %get-tuple-element.518), kind=kOutput, calls=%fused_computation.22.clone.1 | convolution fusion | flops 811991040 | bytes 16261128 | tf_op jit(solution)/shard_map/while/body/eval_jaxpr/grqk,qgrh->kgh/dot_general | solution.py:95
  149.2 17.8 %fusion.116 = f32[1024,2,2,128]{0,3,2,1:T(8,128)S(1)} fusion(f32[1024,2,2,128]{0,3,2,1:T(8,128)S(1)} %copy-done.1, s32[]{:T(128)S(6)} %select_n.100, f32[2,1536,512,2]{2,1,3,0:T(8,128)} %fusion.114, bf16[2048,2,128]{0,2,1:T(8,128)(2,1)} %get-tuple-element.555, s32[]{:T(128)S(6)} %select_n.101, f32[2,2,512,1536]{2,3,1,0:T(8,128)} %get-tuple-element.517, ...), kind=kOutput, calls=%fused_computation.27.clone.1 | convolution fusion | flops 827330048 | bytes 52183048 | tf_op jit(solution)/shard_map/while/body/eval_jaxpr/grqk,kgh->qgrh/dot_general | solution.py:89
  167.0 1.3 copy-done.2
  168.3 1.3 slice.51
  169.6 1.3 collective-permute-start.2
  170.9 1.3 slice.50
  172.2 1.3 collective-permute-start.3
  173.5 1.9 bitcast_multiply_fusion.16
  176.0 1.1 copy-done.3
  177.1 0.6 fusion.78
  178.3 0.6 copy-done.7
  179.0 0.4 fusion.79
  179.5 19.3 %fusion.72 = bf16[5376,1024]{0,1:T(8,128)(2,1)} fusion(bf16[1024,5376]{1,0:T(8,128)(2,1)} %all-gather.2.cloned.1.call-done, bf16[1024,256]{0,1:T(8,128)(2,1)S(1)} %bitcast.154, bf16[1024,256]{0,1:T(8,128)(2,1)S(1)} %bitcast.153, bf16[1024,512]{0,1:T(8,128)(2,1)S(1)} %fusion.78), kind=kOutput, calls=%fused_computation.68 | convolution fusion | flops 11286085632 | bytes 24117248 | tf_op jit(solution)/shard_map/dot_general | solution.py:142
  198.8 1.3 fusion.82
  200.8 160.3 %all-reduce.3.cloned.1.call-done = bf16[5376,1024]{0,1:T(8,128)(2,1)} async-done(((bf16[5376,1024]{0,1:T(8,128)(2,1)}), bf16[5376,1024]{0,1:T(8,128)(2,1)}) %all-reduce.3.cloned.1.call-update) | async-done | bytes 11010064 | tf_op jit(solution)/shard_map/psum | solution.py:148
  361.1 27.2 %conditional.1 = (f32[1,1,1024,1024]{3,2,1,0:T(8,128)}, f32[1,1,1024,1024]{3,2,1,0:T(8,128)}) conditional(s32[]{:T(128)} %convert_element_type.55, () %tuple.63, (bf16[5376,1024]{0,1:T(8,128)(2,1)}, pred[1,6]{1,0:T(4,128)(4,1)S(1)}, s32[6]{0:T(128)S(1)}) %tuple.65), branch_computations={%region_7.8_spmd, %region_8.10_spmd} | conditional | flops 4297064448 | bytes 96469120 | solution.py:176
  361.1 0.6 fusion.67
  362.4 14.6 %copy.36 = bf16[5376,1024]{1,0:T(8,128)(2,1)} copy(bf16[5376,1024]{0,1:T(8,128)(2,1)} %get-tuple-element.421) | data formatting | bytes 22020096 | tf_op jit(solution)/shard_map
  377.1 6.8 %multiply_bitcast_fusion = f32[1,1,1024,1024]{3,2,1,0:T(8,128)} fusion(s32[]{:T(128)S(6)} %select_n.79, bf16[5376,1024]{1,0:T(8,128)(2,1)} %copy.36), kind=kOutput, calls=%fused_computation.59 | convolution fusion | flops 2148532224 | bytes 15204356 | tf_op jit(solution)/shard_map/cond/branch_1_fun/dot_general | solution.py:163
  383.8 4.5 %multiply_bitcast_fusion.1 = f32[1,1,1024,1024]{3,2,1,0:T(8,128)} fusion(s32[]{:T(128)S(6)} %select_n.79, bf16[5376,1024]{1,0:T(8,128)(2,1)S(1)} %copy-done), kind=kOutput, calls=%fused_computation.60 | convolution fusion | flops 2148532224 | bytes 15204356 | tf_op jit(solution)/shard_map/cond/branch_1_fun/dot_general | solution.py:157
  (49 shorter events, 1.6 us)
Async XLA Ops:
  7.2 10.0 %copy-start.10 = (bf16[1024,512]{1,0:T(8,128)(2,1)S(1)}, bf16[1024,512]{1,0:T(8,128)(2,1)}, u32[]{:S(2)}) copy-start(bf16[1024,512]{1,0:T(8,128)(2,1)} %param.12) | copy-start | bytes 3145732
  7.2 172.3 %all-gather.2.cloned.1.call-start = ((), (), s32[]{:S(2)}) async-start(), calls=%async_computation | async-start | bytes 12386304 | tf_op jit(solution)/shard_map/all_gather | solution.py:143
  7.9 353.2 %all-reduce.3.cloned.1.call-start = ((), (), s32[]{:S(2)}) async-start(), calls=%async_computation.1 | async-start | bytes 22020096 | tf_op jit(solution)/shard_map/psum | solution.py:148
  9.2 13.3 %collective-permute-start = (bf16[1024,256]{0,1:T(8,128)(2,1)S(1)}, bf16[1024,256]{0,1:T(8,128)(2,1)}, u32[]{:S(2)}, u32[]{:S(2)}) collective-permute-start(bf16[1024,256]{0,1:T(8,128)(2,1)S(1)} %copy.26), channel_id=1, source_target_pairs={{0,8},{8,16},{16,24},{24,32},{32,40},{40,48},{48,56},{56,64},{64,7... | collective-permute-start | bytes 1572872 | tf_op jit(solution)/shard_map/ppermute | solution.py:23
  12.5 12.1 %collective-permute-start.1 = (bf16[1024,256]{0,1:T(8,128)(2,1)S(1)}, bf16[1024,256]{0,1:T(8,128)(2,1)S(1)}, u32[]{:S(2)}, u32[]{:S(2)}) collective-permute-start(bf16[1024,256]{0,1:T(8,128)(2,1)S(1)} %copy.29), channel_id=1, source_target_pairs={{0,8},{8,16},{16,24},{24,32},{32,40},{40,48},{48,56},{56,64},{64,7... | collective-permute-start | bytes 1572872 | tf_op jit(solution)/shard_map/ppermute | solution.py:23
  24.7 4.8 %copy-start.11 = (s32[1024]{0:T(1024)S(1)}, s32[1024]{0:T(1024)}, u32[]{:S(2)}) copy-start(s32[1024]{0:T(1024)} %param.16) | copy-start | bytes 12292
  42.0 7.6 %copy-start.4 = (f32[2048,2,128]{0,2,1:T(8,128)S(1)}, f32[2048,2,128]{0,2,1:T(8,128)}, u32[]{:S(2)}) copy-start(f32[2048,2,128]{0,2,1:T(8,128)} %get-tuple-element.537) | copy-start | bytes 6291460 | tf_op jit(solution)/shard_map/while
  69.8 1.3 copy-start.5
  71.1 8.7 %copy-start.1 = (f32[1024,2,2,128]{0,3,2,1:T(8,128)S(1)}, f32[1024,2,2,128]{0,3,2,1:T(8,128)}, u32[]{:S(2)}) copy-start(f32[1024,2,2,128]{0,3,2,1:T(8,128)} %get-tuple-element.536) | copy-start | bytes 6291460 | tf_op jit(solution)/shard_map/while
  97.5 1.3 copy-start.2
  111.4 7.6 %copy-start.4 = (f32[2048,2,128]{0,2,1:T(8,128)S(1)}, f32[2048,2,128]{0,2,1:T(8,128)}, u32[]{:S(2)}) copy-start(f32[2048,2,128]{0,2,1:T(8,128)} %get-tuple-element.537) | copy-start | bytes 6291460 | tf_op jit(solution)/shard_map/while
  139.2 1.3 copy-start.5
  140.5 8.7 %copy-start.1 = (f32[1024,2,2,128]{0,3,2,1:T(8,128)S(1)}, f32[1024,2,2,128]{0,3,2,1:T(8,128)}, u32[]{:S(2)}) copy-start(f32[1024,2,2,128]{0,3,2,1:T(8,128)} %get-tuple-element.536) | copy-start | bytes 6291460 | tf_op jit(solution)/shard_map/while
  167.0 1.3 copy-start.2
  169.6 8.1 %collective-permute-start.2 = (bf16[1024,2,128]{0,2,1:T(8,128)(2,1)S(1)}, bf16[1024,2,128]{0,2,1:T(8,128)(2,1)S(1)}, u32[]{:S(2)}, u32[]{:S(2)}) collective-permute-start(bf16[1024,2,128]{0,2,1:T(8,128)(2,1)S(1)} %slice.51), channel_id=1, source_target_pairs={{8,0},{16,8},{24,16},{32,24},{40,32},{48,40},{56,48},{64,56},{72,6... | collective-permute-start | bytes 1572872 | tf_op jit(solution)/shard_map/ppermute | solution.py:23
  172.2 6.0 %collective-permute-start.3 = (bf16[1024,2,128]{0,2,1:T(8,128)(2,1)S(1)}, bf16[1024,2,128]{0,2,1:T(8,128)(2,1)S(1)}, u32[]{:S(2)}, u32[]{:S(2)}) collective-permute-start(bf16[1024,2,128]{0,2,1:T(8,128)(2,1)S(1)} %slice.50), channel_id=1, source_target_pairs={{8,0},{16,8},{24,16},{32,24},{40,32},{48,40},{56,48},{64,56},{72,6... | collective-permute-start | bytes 1572872 | tf_op jit(solution)/shard_map/ppermute | solution.py:23
  175.4 1.6 copy-start.3
  175.4 1.7 copy-start.9
  175.7 2.2 copy-start.6
  175.7 2.2 copy-start.8
  177.1 1.8 copy-start.7
  377.1 6.8 %copy-start = (bf16[5376,1024]{1,0:T(8,128)(2,1)S(1)}, bf16[5376,1024]{1,0:T(8,128)(2,1)}, u32[]{:S(2)}) copy-start(bf16[5376,1024]{1,0:T(8,128)(2,1)} %copy.36) | copy-start | bytes 33030148 | tf_op jit(solution)/shard_map/cond
Sparse Core Ops, SparseCore 0:
  10.3 135.0 all-gather.1
  198.9 162.1 all-reduce.2
where the time goes:
time: 396 us; the launch traced here: 395 us
  matrix products  163 us (41%)
  waiting for transfers between devices  161 us (41%)
  local copies, waits for them, and re-layouts  35.4 us (9%)
  between operations  14.9 us (4%)
  other arithmetic  12.1 us (3%)
  starting transfers between devices  8.32 us (2%)
    psum x1, waiting for transfers between devices, per_device(): gradient = lax.psum(partial_sum.astype(jnp.bfloat16), 'seq')  160 us
    dot_general x2, matrix products, one_block(): jnp.einsum('grqk,qgrh->kgh', grad_score, query_part, preferred_element_ty...  40.5 us
    dot_general x2, matrix products, one_block(): jnp.einsum('grqk,kgh->qgrh', grad_score, key_part, preferred_element_type...  35.5 us
    sub x2, matrix products, one_block(): exponent = jnp.where(allowed, jnp.exp(masked - row_top), 0.0)  23.5 us
    dot_general x1, matrix products, per_device(): lax.dot_general(lax.all_gather(inputs, 'head', axis=0, tiled=True), colum...  19.3 us
    another operation x3, local copies, waits for them, and re-layouts  17.8 us
    dot_general x2, matrix products, one_block(): jnp.einsum('grqk,qgrh->kgh', attend_low, out_part, preferred_element_type...  17.4 us
    dot_general x2, matrix products, one_block(): jnp.einsum('qgrh,kgh->grqk', out_part, value_part, preferred_element_type...  15.1 us
  transfers between devices with their start and end apart: 6, of which 1 were waited for; matrix products, arithmetic and copies ran while one was open for 40% of the time, Pallas kernels for 0%

commit v1 on v0

--- a/solution.py
+++ b/solution.py
@@ -39,6 +39,42 @@
     scaled = gradient * sine_table
     turned = jnp.concatenate([-scaled[..., half_size:], scaled[..., :half_size]], -1)
     return gradient * cosine_table - turned
+
+
+def owned_block(partial, owner_row, block_pick, seq_count):
+    full_blocks = D // BLOCK
+    tail_rows = D - full_blocks * BLOCK
+    piece = BLOCK // seq_count
+    tail_piece = tail_rows // seq_count
+    columns = partial.shape[1]
+    main = partial[: full_blocks * BLOCK].reshape(full_blocks, seq_count, piece, columns)
+    main = main.transpose(1, 0, 2, 3).reshape(seq_count, full_blocks * piece, columns)
+    tail = partial[full_blocks * BLOCK :].reshape(seq_count, tail_piece, columns)
+    arranged = jnp.concatenate([main, tail], 1).reshape(-1, columns)
+    mine = lax.psum_scatter(arranged, "seq", scatter_dimension=0, tiled=True)
+    mine = jnp.concatenate(
+        [mine, jnp.zeros((NBLK * piece - mine.shape[0], columns), mine.dtype)], 0
+    ).reshape(NBLK, piece, columns)
+    destinations = jnp.arange(seq_count, dtype=jnp.int32)
+    dest_block = jnp.sum(
+        jnp.where(
+            owner_row[None, :] == destinations[:, None],
+            jnp.arange(NBLK, dtype=jnp.int32)[None, :],
+            0,
+        ),
+        1,
+    )
+    send = jnp.take(mine, dest_block, axis=0)
+    received = lax.all_to_all(send, "seq", 0, 0, tiled=False)
+    main_block = received.reshape(BLOCK, columns)
+    tail_block = jnp.concatenate(
+        [
+            received[:, :tail_piece].reshape(tail_piece * seq_count, columns),
+            jnp.zeros((BLOCK - tail_piece * seq_count, columns), received.dtype),
+        ],
+        0,
+    )
+    return jnp.where(block_pick == full_blocks, tail_block, main_block)
 
 
 def per_device(inputs, queries, key_rows, values, out_grad, band_start, owners):
@@ -145,13 +181,10 @@
         (((0,), (0,)), ((), ())),
         preferred_element_type=jnp.float32,
     )
-    gradient = lax.psum(partial_sum.astype(jnp.bfloat16), "seq")
-    padded = jnp.pad(gradient, ((0, NBLK * BLOCK - D), (0, 0)))
     owner_row = lax.dynamic_index_in_dim(owners, group_index, 0, keepdims=False)
     is_mine = owner_row == seq_index
     block_pick = jnp.sum(jnp.where(is_mine, jnp.arange(NBLK, dtype=jnp.int32), 0))
-    block_part = lax.dynamic_slice_in_dim(padded, block_pick * BLOCK, BLOCK, 0)
-
+    block_part = owned_block(partial_sum.astype(jnp.bfloat16), owner_row, block_pick, seq_count)
     def gram_pair(part_rows):
         left_value = (
             lax.dot_general(

time: 396 us -> 390 us (0.985)
  waiting for transfers between devices: 161 us -> 118 us
  local copies, waits for them, and re-layouts: 35.4 us -> 56 us
  other arithmetic: 12.1 us -> 26.4 us
    psum x1 -> x0, waiting for transfers between devices: 160 us -> none  [per_device(): gradient = lax.psum(partial_sum.astype(jnp.bfloat16), 'seq')]
    reduce_scatter x0 -> x1, waiting for transfers between devices: none -> 89.8 us  [owned_block(): mine = lax.psum_scatter(arranged, 'seq', scatter_dimension=0, tiled=True)]
    all_to_all x0 -> x1, waiting for transfers between devices: none -> 27.3 us  [owned_block(): received = lax.all_to_all(send, 'seq', 0, 0, tiled=False)]
    slice x0 -> x6, local copies, waits for them, and re-layouts: none -> 23.2 us  [the longest x2 22.9 us: owned_block(): partial[:full_blocks * BLOCK]]
    another operation x3 -> x2, local copies, waits for them, and re-layouts: 17.8 us -> 3.14 us
    concatenate x0 -> x1, other arithmetic: none -> 11.8 us  [owned_block(): arranged = jnp.concatenate([main, tail], 1).reshape(-1, columns)]
    transpose x0 -> x1, local copies, waits for them, and re-layouts: none -> 10.2 us  [owned_block(): main.transpose(1, 0, 2, 3).reshape(seq_count, full_blocks * piece, columns)]
  transfers between devices with their start and end apart: 6 -> 7, of which waited for: 1 -> 2; matrix products, arithmetic and copies ran while one was open for 40% -> 40% of each run, Pallas kernels for 0% -> 0%
where the time goes in v1:
time: 390 us; the launch traced here: 388 us
  matrix products  160 us (41%)
  waiting for transfers between devices  118 us (30%)
  local copies, waits for them, and re-layouts  56 us (14%)
  other arithmetic  26.4 us (7%)
  between operations  14.9 us (4%)
  starting transfers between devices  12 us (3%)
    reduce_scatter x1, waiting for transfers between devices, owned_block(): mine = lax.psum_scatter(arranged, 'seq', scatter_dimension=0, tiled=True)  89.8 us
    dot_general x2, matrix products, one_block(): jnp.einsum('grqk,qgrh->kgh', grad_score, query_part, preferred_element_ty...  40.5 us
    dot_general x2, matrix products, one_block(): jnp.einsum('grqk,kgh->qgrh', grad_score, key_part, preferred_element_type...  35.5 us
    all_to_all x1, waiting for transfers between devices, owned_block(): received = lax.all_to_all(send, 'seq', 0, 0, tiled=False)  27.3 us
    sub x2, matrix products, one_block(): exponent = jnp.where(allowed, jnp.exp(masked - row_top), 0.0)  23.5 us
    slice x2, local copies, waits for them, and re-layouts, owned_block(): partial[:full_blocks * BLOCK]  22.9 us
    dot_general x1, matrix products, per_device(): lax.dot_general(lax.all_gather(inputs, 'head', axis=0, tiled=True), colum...  19.4 us
    dot_general x2, matrix products, one_block(): jnp.einsum('grqk,qgrh->kgh', attend_low, out_part, preferred_element_type...  17.4 us
  transfers between devices with their start and end apart: 7, of which 2 were waited for; matrix products, arithmetic and copies ran while one was open for 40% of the time, Pallas kernels for 0%

profile of v1, /device:TPU:0, one launch (start us, length us, event | category | flops | bytes accessed | tf_op | source)
XLA Modules:
  0.0 388.2 jit_solution(11764302622407252420)
XLA Ops:
  8.0 1.2 copy.45
  9.2 2.1 collective-permute-start
  11.3 1.2 copy.48
  12.5 3.6 collective-permute-start.1
  16.2 1.0 multiply_cosine_fusion
  17.2 1.3 copy.47
  18.5 2.3 copy.50
  20.8 0.9 pad_maximum_fusion.5
  21.6 0.9 pad_maximum_fusion.4
  22.5 2.2 pad_maximum_fusion.2
  24.8 1.6 broadcast.113
  26.3 1.6 broadcast.113.clone
  27.9 1.6 broadcast_in_dim.120
  29.5 138.9 %while.22 = (s32[]{:T(128)}, f32[1024,2,2,128]{0,3,2,1:T(8,128)}, f32[2048,2,128]{0,2,1:T(8,128)}, f32[2048,2,128]{0,2,1:T(8,128)}, bf16[2048,2,128]{0,2,1:T(8,1...) while((s32[]{:T(128)}, f32[1024,2,2,128]{0,3,2,1:T(8,128)}, ...), condition=%wide.region_6.7_spmd, body=%wide.region_2.6_spmd.sunk | while | flops 4095748608 | bytes 186194320 | solution.py:154
  30.3 11.8 %fusion.115 = (f32[2,2,512]{2,1,0:T(2,128)S(1)}, f32[2,2,512,1536]{2,3,1,0:T(8,128)}) fusion(pred[512,1536]{0,1:T(8,128)(4,1)S(1)} %compare_and_fusion.3, bf16[2048,2,128]{0,2,1:T(8,128)(2,1)} %get-tuple-element.532, s32[]{:T(128)S(6)} %select_n.140, bf16[1024,2,2,128]{0,3,2,1:T(8,128)(2,1)} %get-tuple-element.535, s32[]{:T(128)S(6)} %select_n.139), kind=kOutput, calls=%fused_computation.105.clone.1 | convolution fusion | flops 821036544 | bytes 15474696 | tf_op jit(solution)/shard_map/while/body/eval_jaxpr/sub | solution.py:117
  42.0 7.6 %fusion.114 = f32[2,1536,512,2]{2,1,3,0:T(8,128)} fusion(bf16[2048,2,128]{0,2,1:T(8,128)(2,1)S(1)} %get-tuple-element.536, s32[]{:T(128)S(6)} %select_n.140, bf16[1024,2,2,128]{0,3,2,1:T(8,128)(2,1)} %get-tuple-element.537, s32[]{:T(128)S(6)} %select_n.139), kind=kOutput, calls=%fused_computation.34.clone.1 | convolution fusion | flops 805306368 | bytes 13893640 | tf_op jit(solution)/shard_map/while/body/eval_jaxpr/qgrh,kgh->grqk/dot_general | solution.py:120
  49.6 20.2 %fusion.117 = f32[2048,2,128]{0,2,1:T(8,128)S(1)} fusion(f32[2048,2,128]{0,2,1:T(8,128)S(1)} %copy-done.3, s32[]{:T(128)S(6)} %select_n.140, f32[2,1536,512,2]{2,1,3,0:T(8,128)} %fusion.114, bf16[1024,2,2,128]{0,3,2,1:T(8,128)(2,1)} %get-tuple-element.535, s32[]{:T(128)S(6)} %select_n.139, f32[2,2,512,1536]{2,3,1,0:T(8,128)} %get-tuple-element.494, ...), kind=kOutput, calls=%fused_computation.26.clone.1 | convolution fusion | flops 827723264 | bytes 54018056 | tf_op jit(solution)/shard_map/while/body/eval_jaxpr/grqk,qgrh->kgh/dot_general | solution.py:128
  69.8 1.3 copy-done.4
  71.1 8.7 %fusion.118 = f32[2048,2,128]{0,2,1:T(8,128)} fusion(f32[2048,2,128]{0,2,1:T(8,128)} %get-tuple-element.515, s32[]{:T(128)S(6)} %select_n.140, bf16[1024,2,2,128]{0,3,2,1:T(8,128)(2,1)} %get-tuple-element.537, s32[]{:T(128)S(6)} %select_n.139, f32[2,2,512,1536]{2,3,1,0:T(8,128)} %get-tuple-element.494, f32[2,2,512]{2,1,0:T(2,128)S(1)} %get-tuple-element.495), kind=kOutput, calls=%fused_computation.23.clone.1 | convolution fusion | flops 811991040 | bytes 16261128 | tf_op jit(solution)/shard_map/while/body/eval_jaxpr/grqk,qgrh->kgh/dot_general | solution.py:131
  79.8 17.7 %fusion.116 = f32[1024,2,2,128]{0,3,2,1:T(8,128)S(1)} fusion(f32[1024,2,2,128]{0,3,2,1:T(8,128)S(1)} %copy-done, s32[]{:T(128)S(6)} %select_n.139, f32[2,1536,512,2]{2,1,3,0:T(8,128)} %fusion.114, bf16[2048,2,128]{0,2,1:T(8,128)(2,1)} %get-tuple-element.532, s32[]{:T(128)S(6)} %select_n.140, f32[2,2,512,1536]{2,3,1,0:T(8,128)} %get-tuple-element.494, ...), kind=kOutput, calls=%fused_computation.28.clone.1 | convolution fusion | flops 827330048 | bytes 52183048 | tf_op jit(solution)/shard_map/while/body/eval_jaxpr/grqk,kgh->qgrh/dot_general | solution.py:125
  97.6 1.3 copy-done.1
  99.7 11.7 %fusion.115 = (f32[2,2,512]{2,1,0:T(2,128)S(1)}, f32[2,2,512,1536]{2,3,1,0:T(8,128)}) fusion(pred[512,1536]{0,1:T(8,128)(4,1)S(1)} %compare_and_fusion.3, bf16[2048,2,128]{0,2,1:T(8,128)(2,1)} %get-tuple-element.532, s32[]{:T(128)S(6)} %select_n.140, bf16[1024,2,2,128]{0,3,2,1:T(8,128)(2,1)} %get-tuple-element.535, s32[]{:T(128)S(6)} %select_n.139), kind=kOutput, calls=%fused_computation.105.clone.1 | convolution fusion | flops 821036544 | bytes 15474696 | tf_op jit(solution)/shard_map/while/body/eval_jaxpr/sub | solution.py:117
  111.4 7.6 %fusion.114 = f32[2,1536,512,2]{2,1,3,0:T(8,128)} fusion(bf16[2048,2,128]{0,2,1:T(8,128)(2,1)S(1)} %get-tuple-element.536, s32[]{:T(128)S(6)} %select_n.140, bf16[1024,2,2,128]{0,3,2,1:T(8,128)(2,1)} %get-tuple-element.537, s32[]{:T(128)S(6)} %select_n.139), kind=kOutput, calls=%fused_computation.34.clone.1 | convolution fusion | flops 805306368 | bytes 13893640 | tf_op jit(solution)/shard_map/while/body/eval_jaxpr/qgrh,kgh->grqk/dot_general | solution.py:120
  118.9 20.2 %fusion.117 = f32[2048,2,128]{0,2,1:T(8,128)S(1)} fusion(f32[2048,2,128]{0,2,1:T(8,128)S(1)} %copy-done.3, s32[]{:T(128)S(6)} %select_n.140, f32[2,1536,512,2]{2,1,3,0:T(8,128)} %fusion.114, bf16[1024,2,2,128]{0,3,2,1:T(8,128)(2,1)} %get-tuple-element.535, s32[]{:T(128)S(6)} %select_n.139, f32[2,2,512,1536]{2,3,1,0:T(8,128)} %get-tuple-element.494, ...), kind=kOutput, calls=%fused_computation.26.clone.1 | convolution fusion | flops 827723264 | bytes 54018056 | tf_op jit(solution)/shard_map/while/body/eval_jaxpr/grqk,qgrh->kgh/dot_general | solution.py:128
  139.2 1.3 copy-done.4
  140.5 8.7 %fusion.118 = f32[2048,2,128]{0,2,1:T(8,128)} fusion(f32[2048,2,128]{0,2,1:T(8,128)} %get-tuple-element.515, s32[]{:T(128)S(6)} %select_n.140, bf16[1024,2,2,128]{0,3,2,1:T(8,128)(2,1)} %get-tuple-element.537, s32[]{:T(128)S(6)} %select_n.139, f32[2,2,512,1536]{2,3,1,0:T(8,128)} %get-tuple-element.494, f32[2,2,512]{2,1,0:T(2,128)S(1)} %get-tuple-element.495), kind=kOutput, calls=%fused_computation.23.clone.1 | convolution fusion | flops 811991040 | bytes 16261128 | tf_op jit(solution)/shard_map/while/body/eval_jaxpr/grqk,qgrh->kgh/dot_general | solution.py:131
  149.2 17.8 %fusion.116 = f32[1024,2,2,128]{0,3,2,1:T(8,128)S(1)} fusion(f32[1024,2,2,128]{0,3,2,1:T(8,128)S(1)} %copy-done, s32[]{:T(128)S(6)} %select_n.139, f32[2,1536,512,2]{2,1,3,0:T(8,128)} %fusion.114, bf16[2048,2,128]{0,2,1:T(8,128)(2,1)} %get-tuple-element.532, s32[]{:T(128)S(6)} %select_n.140, f32[2,2,512,1536]{2,3,1,0:T(8,128)} %get-tuple-element.494, ...), kind=kOutput, calls=%fused_computation.28.clone.1 | convolution fusion | flops 827330048 | bytes 52183048 | tf_op jit(solution)/shard_map/while/body/eval_jaxpr/grqk,kgh->qgrh/dot_general | solution.py:125
  167.0 1.3 copy-done.1
  168.3 1.3 slice.67
  169.6 1.3 collective-permute-start.2
  170.9 1.3 slice.66
  172.2 1.3 collective-permute-start.3
  173.5 1.9 bitcast_multiply_fusion.16
  176.0 1.1 copy-done.2
  179.5 19.4 %fusion.67 = bf16[5376,1024]{0,1:T(8,128)(2,1)} fusion(bf16[1024,5376]{1,0:T(8,128)(2,1)} %all-gather.2.cloned.1.call-done, bf16[1024,256]{0,1:T(8,128)(2,1)S(1)} %bitcast.177, bf16[1024,256]{0,1:T(8,128)(2,1)S(1)} %bitcast.176, bf16[1024,512]{0,1:T(8,128)(2,1)S(1)} %fusion.73), kind=kOutput, calls=%fused_computation.65 | convolution fusion | flops 11286085632 | bytes 24117248 | tf_op jit(solution)/shard_map/dot_general | solution.py:178
  198.9 8.5 %slice.54 = bf16[5120,1024]{0,1:T(8,128)(2,1)} slice(bf16[5376,1024]{0,1:T(8,128)(2,1)} %fusion.67), slice={[0:5120], [0:1024]} | slice | bytes 20971520 | tf_op jit(solution)/shard_map/slice | solution.py:50
  207.4 14.4 %copy.55 = bf16[5120,1024]{1,0:T(8,128)(2,1)} copy(bf16[5120,1024]{0,1:T(8,128)(2,1)} %slice.54) | data formatting | bytes 20971520 | tf_op jit(solution)/shard_map/slice | solution.py:50
  221.8 10.2 %copy.56 = bf16[16,5,64,1024]{3,2,1,0:T(8,128)(2,1)} copy(bf16[16,5,64,1024]{3,2,0,1:T(8,128)(2,1)} %bitcast.171) | data formatting | bytes 20971520 | tf_op jit(solution)/shard_map/transpose | solution.py:51
  232.2 11.8 %pad_maximum_fusion = bf16[16,336,1024]{2,1,0:T(8,128)(2,1)} fusion(bf16[16,16,1024]{2,1,0:T(8,128)(2,1)S(1)} %bitcast.175, bf16[16,320,1024]{2,1,0:T(8,128)(2,1)} %bitcast.170), kind=kLoop, calls=%fused_computation.64 | loop fusion | flops 22020096 | bytes 22020096 | tf_op jit(solution)/shard_map/concatenate | solution.py:53
  244.1 1.3 fusion.78
  245.5 89.8 %reduce-scatter.2.cloned.1.call-done = bf16[336,1024]{1,0:T(8,128)(2,1)} async-done(((bf16[5376,1024]{1,0:T(8,128)(2,1)}), bf16[336,1024]{1,0:T(8,128)(2,1)}) %reduce-scatter.2.cloned.1.call-update) | async-done | bytes 688144 | tf_op jit(solution)/shard_map/reduce_scatter | solution.py:54
  335.3 1.2 concatenate.42
  337.2 1.6 broadcast_select_fusion
  338.8 3.7 all-to-all-start
  343.1 27.3 %all-to-all-done = bf16[16,64,1024]{2,1,0:T(8,128)(2,1)S(1)} async-done(((bf16[16,64,1024]{2,1,0:T(8,128)(2,1)}), bf16[16,64,1024]{2,1,0:T(8,128)(2,1)S(1)}, u32[]{:S(2)}, u32[]{:S(2)}) %all-to-all-start) | async-done | bytes 2097184 | tf_op jit(solution)/shard_map/all_to_all | solution.py:68
  370.4 10.9 %conditional.1 = (f32[1,1,1024,1024]{3,2,1,0:T(8,128)}, f32[1,1,1024,1024]{3,2,1,0:T(8,128)}) conditional(s32[]{:T(128)} %convert_element_type.53, () %tuple.53, (pred[6]{0:T(512)(128)(4,1)S(1)}, s32[6]{0:T(128)S(1)}, bf16[16,64,1024]{2,1,0:T(8,128)(2,1)S(1)}) %tuple.55), branch_computations={%region_8.9_spmd, %region_9.11_spmd} | conditional | flops 4298113024 | bytes 18350140 | solution.py:209
  372.5 4.4 %multiply_bitcast_fusion = f32[1,1,1024,1024]{3,2,1,0:T(8,128)} fusion(bf16[1024,1024]{1,0:T(8,128)(2,1)S(1)} %bitcast_select_fusion.4), kind=kOutput, calls=%fused_computation.59 | convolution fusion | flops 2148532224 | bytes 6291456 | tf_op jit(solution)/shard_map/cond/branch_1_fun/dot_general | solution.py:196
  376.9 4.4 %multiply_bitcast_fusion.1 = f32[1,1,1024,1024]{3,2,1,0:T(8,128)} fusion(bf16[1024,1024]{1,0:T(8,128)(2,1)S(1)} %bitcast_select_fusion.4), kind=kOutput, calls=%fused_computation.60 | convolution fusion | flops 2148532224 | bytes 6291456 | tf_op jit(solution)/shard_map/cond/branch_1_fun/dot_general | solution.py:190
  (64 shorter events, 7.7 us)
Async XLA Ops:
  7.2 10.0 %copy-start.9 = (bf16[1024,512]{1,0:T(8,128)(2,1)S(1)}, bf16[1024,512]{1,0:T(8,128)(2,1)}, u32[]{:S(2)}) copy-start(bf16[1024,512]{1,0:T(8,128)(2,1)} %param.12) | copy-start | bytes 3145732
  7.2 172.3 %all-gather.2.cloned.1.call-start = ((), (), s32[]{:S(2)}) async-start(), calls=%async_computation.2 | async-start | bytes 12386304 | tf_op jit(solution)/shard_map/all_gather | solution.py:179
  7.9 327.4 %reduce-scatter.2.cloned.1.call-start = ((), (), s32[]{:S(2)}) async-start(), calls=%async_computation.3 | async-start | bytes 11698176 | tf_op jit(solution)/shard_map/reduce_scatter | solution.py:54
  9.2 13.3 %collective-permute-start = (bf16[1024,256]{0,1:T(8,128)(2,1)S(1)}, bf16[1024,256]{0,1:T(8,128)(2,1)}, u32[]{:S(2)}, u32[]{:S(2)}) collective-permute-start(bf16[1024,256]{0,1:T(8,128)(2,1)S(1)} %copy.45), channel_id=1, source_target_pairs={{0,8},{8,16},{16,24},{24,32},{32,40},{40,48},{48,56},{56,64},{64,7... | collective-permute-start | bytes 1572872 | tf_op jit(solution)/shard_map/ppermute | solution.py:23
  12.5 12.1 %collective-permute-start.1 = (bf16[1024,256]{0,1:T(8,128)(2,1)S(1)}, bf16[1024,256]{0,1:T(8,128)(2,1)S(1)}, u32[]{:S(2)}, u32[]{:S(2)}) collective-permute-start(bf16[1024,256]{0,1:T(8,128)(2,1)S(1)} %copy.48), channel_id=1, source_target_pairs={{0,8},{8,16},{16,24},{24,32},{32,40},{40,48},{48,56},{56,64},{64,7... | collective-permute-start | bytes 1572872 | tf_op jit(solution)/shard_map/ppermute | solution.py:23
  24.7 4.8 %copy-start.10 = (s32[1024]{0:T(1024)S(1)}, s32[1024]{0:T(1024)}, u32[]{:S(2)}) copy-start(s32[1024]{0:T(1024)} %param.16) | copy-start | bytes 12292
  42.0 7.6 %copy-start.3 = (f32[2048,2,128]{0,2,1:T(8,128)S(1)}, f32[2048,2,128]{0,2,1:T(8,128)}, u32[]{:S(2)}) copy-start(f32[2048,2,128]{0,2,1:T(8,128)} %get-tuple-element.514) | copy-start | bytes 6291460 | tf_op jit(solution)/shard_map/while
  69.8 1.3 copy-start.4
  71.1 8.7 %copy-start = (f32[1024,2,2,128]{0,3,2,1:T(8,128)S(1)}, f32[1024,2,2,128]{0,3,2,1:T(8,128)}, u32[]{:S(2)}) copy-start(f32[1024,2,2,128]{0,3,2,1:T(8,128)} %get-tuple-element.513) | copy-start | bytes 6291460 | tf_op jit(solution)/shard_map/while
  97.6 1.3 copy-start.1
  111.4 7.6 %copy-start.3 = (f32[2048,2,128]{0,2,1:T(8,128)S(1)}, f32[2048,2,128]{0,2,1:T(8,128)}, u32[]{:S(2)}) copy-start(f32[2048,2,128]{0,2,1:T(8,128)} %get-tuple-element.514) | copy-start | bytes 6291460 | tf_op jit(solution)/shard_map/while
  139.2 1.3 copy-start.4
  140.5 8.7 %copy-start = (f32[1024,2,2,128]{0,3,2,1:T(8,128)S(1)}, f32[1024,2,2,128]{0,3,2,1:T(8,128)}, u32[]{:S(2)}) copy-start(f32[1024,2,2,128]{0,3,2,1:T(8,128)} %get-tuple-element.513) | copy-start | bytes 6291460 | tf_op jit(solution)/shard_map/while
  167.0 1.3 copy-start.1
  169.6 8.1 %collective-permute-start.2 = (bf16[1024,2,128]{0,2,1:T(8,128)(2,1)S(1)}, bf16[1024,2,128]{0,2,1:T(8,128)(2,1)S(1)}, u32[]{:S(2)}, u32[]{:S(2)}) collective-permute-start(bf16[1024,2,128]{0,2,1:T(8,128)(2,1)S(1)} %slice.67), channel_id=1, source_target_pairs={{8,0},{16,8},{24,16},{32,24},{40,32},{48,40},{56,48},{64,56},{72,6... | collective-permute-start | bytes 1572872 | tf_op jit(solution)/shard_map/ppermute | solution.py:23
  172.2 6.1 %collective-permute-start.3 = (bf16[1024,2,128]{0,2,1:T(8,128)(2,1)S(1)}, bf16[1024,2,128]{0,2,1:T(8,128)(2,1)S(1)}, u32[]{:S(2)}, u32[]{:S(2)}) collective-permute-start(bf16[1024,2,128]{0,2,1:T(8,128)(2,1)S(1)} %slice.66), channel_id=1, source_target_pairs={{8,0},{16,8},{24,16},{32,24},{40,32},{48,40},{56,48},{64,56},{72,6... | collective-permute-start | bytes 1572872 | tf_op jit(solution)/shard_map/ppermute | solution.py:23
  175.4 1.6 copy-start.2
  175.4 1.7 copy-start.8
  175.7 2.2 copy-start.5
  175.7 2.2 copy-start.7
  177.1 1.8 copy-start.6
  221.8 10.2 %slice-start = ((bf16[5376,1024]{0,1:T(8,128)(2,1)}), bf16[256,1024]{0,1:T(8,128)(2,1)S(1)}, s32[]{:S(2)}) async-start(bf16[5376,1024]{0,1:T(8,128)(2,1)} %fusion.67), calls=%async_computation.4 | async-start | bytes 1048576 | tf_op jit(solution)/shard_map/slice | solution.py:52
  338.8 31.7 %all-to-all-start = ((bf16[16,64,1024]{2,1,0:T(8,128)(2,1)}), bf16[16,64,1024]{2,1,0:T(8,128)(2,1)S(1)}, u32[]{:S(2)}, u32[]{:S(2)}) async-start(bf16[16,64,1024]{2,1,0:T(8,128)(2,1)} %broadcast_select_fusion), calls=%async_computation.1 | async-start | bytes 4194304 | tf_op jit(solution)/shard_map/all_to_all | solution.py:68
Sparse Core Ops, SparseCore 0:
  10.3 135.0 all-gather.1
  244.2 91.0 reduce-scatter.1
